TPU v7x, 512 devices: a whole 4x4x16 slice. The times are simulated.
512 devices in a mesh: comp: 32 (over z, core), feat: 16 (over x, y).
Axes of the slice: x: 4, y: 4, z: 16, core: 2. Of those that a mesh axis runs over, the one named last changes fastest.
Arguments:
- block_values: bfloat16 [32, 16, 24, 128, 128], P('comp', 'feat'), may hold values from -0.0625 to 0.0625
- block_rows: int32 [32, 16, 24], P('comp', 'feat'), may hold values from 0 to 15, as said below
- block_cols: int32 [32, 16, 24], P('comp', 'feat'), may hold values from 0 to 13, as said below
- block_counts: int32 [32, 16], P('comp', 'feat'), may hold values from 8 to 24, as said below
- right_side: float32 [65536, 128], P(('comp', 'feat')), may hold values from -6 to 6
- ridge: float32 [128], replicated, may hold values from 0.1 to 2
Outputs:
- solution: float32 [28672, 128], P('feat')
- residual: float32 [65536, 128], P(('comp', 'feat'))
Inputs may be any that keep to these rules, and one draw needn't show every extreme that they name: Within one device the listed (block_rows, block_cols) pairs of all 24 slots are distinct; block rows are very uneven in how many blocks they hold. `block_cols`: see block_rows. `block_counts`: slots at or beyond a device's count are ignored; some device is full in every draw.
All inputs are finite; a program needn't handle non-finite values.
Results may differ from a plain program's by a relative error of at most 0.0029.
Values may be sent and summed in bfloat16 or wider, within the bound.
No kernel may reach another device: no remote copies, remote signals or barrier semaphores. Data moves between devices by JAX's collectives and lax.ppermute only.
A program may use at most 64 MiB of HBM per device.

v0:
```python
import jax
import jax.numpy as jnp
from jax import lax
from jax.sharding import PartitionSpec as P

RB_DEV = 16
CB_DEV = 14
ITERS = 2


def reduce_over(partial, axis, parts):
    rows = partial.shape[0] // parts
    pieces = partial.reshape(parts, rows, *partial.shape[1:])
    return lax.all_to_all(pieces, axis, 0, 0, tiled=True).sum(0)


def total_over_mesh(stacked, n_comp, n_feat):
    spread = jnp.broadcast_to(stacked[None], (n_feat,) + stacked.shape)
    by_feat = lax.all_to_all(spread, "feat", 0, 0, tiled=True).sum(0)
    spread = jnp.broadcast_to(by_feat[None], (n_comp,) + stacked.shape)
    return lax.all_to_all(spread, "comp", 0, 0, tiled=True).sum(0)


def shards(block_values, block_rows, block_cols, block_counts, right_side, ridge, n_comp, n_feat):
    values = block_values[0, 0]
    slot_rows = block_rows[0, 0]
    slot_cols = block_cols[0, 0]
    count_of_slots = block_counts[0, 0]
    responses = right_side.shape[1]
    total_slot_number = values.shape[0]
    block_edge = values.shape[1]
    feat_rows = CB_DEV * block_edge
    own_rows = feat_rows // n_comp
    comp_index = lax.axis_index("comp")
    slot_live = (jnp.arange(total_slot_number) < count_of_slots).astype(jnp.float32)
    row_lookup_table = (jnp.arange(RB_DEV)[:, None] == slot_rows[None, :]).astype(
        jnp.float32
    ) * slot_live[None, :]
    col_table = (jnp.arange(CB_DEV)[:, None] == slot_cols[None, :]).astype(jnp.float32) * slot_live[
        None, :
    ]

    def backward(low_slab):
        row_slabs = low_slab.reshape(RB_DEV, block_edge, responses)
        selected = jnp.take(row_slabs, slot_rows, axis=0)
        block_products = jnp.einsum(
            "sij,sik->sjk", values, selected, preferred_element_type=jnp.float32
        )
        summed = jnp.einsum(
            "qs,sjk->qjk", col_table, block_products, precision=lax.Precision.HIGHEST
        )
        return summed.reshape(feat_rows, responses)

    def forward(direction):
        col_panels = direction.astype(jnp.bfloat16).reshape(CB_DEV, block_edge, responses)
        forward_selected = jnp.take(col_panels, slot_cols, axis=0)
        forward_block_products = jnp.einsum(
            "sij,sjk->sik", values, forward_selected, preferred_element_type=jnp.float32
        )
        forward_summed = jnp.einsum(
            "rs,sik->rik", row_lookup_table, forward_block_products, precision=lax.Precision.HIGHEST
        )
        return reduce_over(forward_summed.reshape(RB_DEV * block_edge, responses), "feat", n_feat)

    def slab_of(current):
        return lax.all_gather(current.astype(jnp.bfloat16), "feat", axis=0, tiled=True)

    core = comp_index % 2
    half_rows = feat_rows // 2
    part_rows = half_rows // n_comp
    siblings = [(i, i ^ 1) for i in range(n_comp)]

    def gradient_rows(current):
        partial = backward(slab_of(current))
        kept = lax.dynamic_slice_in_dim(partial, core * half_rows, half_rows, axis=0)
        sent = lax.dynamic_slice_in_dim(partial, (1 - core) * half_rows, half_rows, axis=0)
        chip_sum = kept + lax.ppermute(sent, "comp", siblings)
        pieces = chip_sum.reshape(n_comp, part_rows, chip_sum.shape[1])
        landed = lax.all_to_all(pieces, "comp", 0, 0, tiled=True)
        halves = landed.reshape(n_comp // 2, 2, part_rows, chip_sum.shape[1]).sum(0)
        return halves.reshape(own_rows, chip_sum.shape[1])

    def whole_of(gathered):
        split = gathered.reshape(n_comp, 2, part_rows, gathered.shape[-1])
        return split.transpose(1, 0, 2, 3).reshape(feat_rows, gathered.shape[-1])

    def own_part(full):
        split = full.reshape(2, n_comp, part_rows, full.shape[-1])
        mine = lax.dynamic_slice_in_dim(split, comp_index, 1, axis=1)
        return mine.reshape(own_rows, full.shape[-1])

    def col_sq(x):
        return jnp.sum(x * x, axis=0)

    residual = right_side
    gradient_own = gradient_rows(residual)
    direction = whole_of(lax.all_gather(gradient_own, "comp", axis=0, tiled=False))
    image_rows = forward(direction)
    energy, image_energy = total_over_mesh(
        jnp.stack([col_sq(gradient_own), col_sq(image_rows)]), n_comp, n_feat
    )
    step_size = energy / (image_energy + ridge * energy)
    solution = step_size * direction
    residual = residual - step_size * image_rows
    for _ in range(1, ITERS):
        gradient_own = gradient_rows(residual) - ridge * own_part(solution)
        gathered = lax.all_gather(
            jnp.concatenate([gradient_own, col_sq(gradient_own)[None]], axis=0),
            "comp",
            axis=0,
            tiled=False,
        )
        gradient = whole_of(gathered[:, :own_rows])
        comp_energy = jnp.sum(gathered[:, own_rows], axis=0)
        spread = jnp.broadcast_to(comp_energy[None, None], (n_feat, 1, responses))
        next_energy = lax.all_to_all(spread, "feat", 0, 0, tiled=True).sum(0)[0]
        direction = gradient + next_energy / energy * direction
        energy = next_energy
        image_rows = forward(direction)
        image_energy, direction_energy = total_over_mesh(
            jnp.stack([col_sq(image_rows), col_sq(own_part(direction))]), n_comp, n_feat
        )
        step_size = energy / (image_energy + ridge * direction_energy)
        solution = solution + step_size * direction
        residual = residual - step_size * image_rows
    return (solution, residual)


def solution(mesh):
    placed = (
        P("comp", "feat", None, None, None),
        P("comp", "feat", None),
        P("comp", "feat", None),
        P("comp", "feat"),
        P(("comp", "feat"), None),
        P(),
    )
    n_comp = mesh.shape["comp"]
    n_feat = mesh.shape["feat"]

    def body(*args):
        return shards(*args, n_comp=n_comp, n_feat=n_feat)

    return jax.shard_map(
        body,
        mesh=mesh,
        in_specs=placed,
        out_specs=(P("feat", None), P(("comp", "feat"), None)),
        check_vma=False,
    )
```

profile of v0, /device:TPU:1, one launch (start us, length us, event | category | flops | bytes accessed | tf_op | source)
XLA Modules:
  0.0 364.6 jit_solution(9498467656124753706)
XLA Ops:
  3.6 20.0 %all_gather.15 = bf16[2048,128]{1,0:T(8,128)(2,1)S(1)} all-gather(bf16[128,128]{1,0:T(8,128)(2,1)S(1)} %convert_element_type.24), channel_id=1, replica_groups=mesh['comp'=32,'feat'=16] {'feat'}, dimensions={0}, use_global_device_ids=true | all-gather | bytes 557056 | tf_op jit(solution)/shard_map/all_gather | solution.py:66
  29.3 9.8 %collective-permute-start = (f32[896,128]{1,0:T(8,128)S(1)}, f32[896,128]{1,0:T(8,128)S(1)}, u32[]{:S(2)}, u32[]{:S(2)}) collective-permute-start(f32[896,128]{1,0:T(8,128)S(1)} %constant_dynamic-slice_fusion.1), channel_id=1, source_target_pairs={{0,16},{16,0},{32,48},{48,32},{64,80},{80,64},{96,112},{112,96},{1... | collective-permute-start | bytes 1376264 | tf_op jit(solution)/shard_map/ppermute | solution.py:77
  41.5 13.5 %all-to-all-start = ((f32[32,28,128]{2,1,0:T(8,128)}), f32[32,28,128]{2,1,0:T(8,128)S(1)}, u32[]{:S(2)}, u32[]{:S(2)}) async-start(f32[32,28,128]{2,1,0:T(8,128)} %reshape.111), calls=%async_computation | async-start | bytes 1048576 | tf_op jit(solution)/shard_map/all_to_all | solution.py:79
  55.0 33.5 %all-to-all-done = f32[32,28,128]{2,1,0:T(8,128)S(1)} async-done(((f32[32,28,128]{2,1,0:T(8,128)}), f32[32,28,128]{2,1,0:T(8,128)S(1)}, u32[]{:S(2)}, u32[]{:S(2)}) %all-to-all-start) | async-done | bytes 458784 | tf_op jit(solution)/shard_map/all_to_all | solution.py:79
  88.5 29.8 %all_gather.16 = f32[32,56,128]{2,1,0:T(8,128)S(1)} all-gather(f32[1,56,128]{2,1,0:T(8,128)S(1)} %all_gather_reshape.3), channel_id=1, replica_groups=mesh['comp'=32,'feat'=16] {'comp'}, dimensions={0}, use_global_device_ids=true | all-gather | bytes 946176 | tf_op jit(solution)/shard_map/all_gather | solution.py:97
  121.7 3.1 convolution_bitcast_fusion.2
  124.8 3.0 copy.96
  131.6 4.8 %all-to-all-start.1 = ((f32[16,128,128]{2,1,0:T(8,128)}), f32[16,128,128]{2,1,0:T(8,128)S(1)}, u32[]{:S(2)}, u32[]{:S(2)}) async-start(f32[16,128,128]{2,1,0:T(8,128)} %copy.97), calls=%async_computation.1 | async-start | bytes 2097152 | tf_op jit(solution)/shard_map/all_to_all | solution.py:14
  136.4 16.1 %all-to-all-done.1 = f32[16,128,128]{2,1,0:T(8,128)S(1)} async-done(((f32[16,128,128]{2,1,0:T(8,128)}), f32[16,128,128]{2,1,0:T(8,128)S(1)}, u32[]{:S(2)}, u32[]{:S(2)}) %all-to-all-start.1) | async-done | bytes 1048608 | tf_op jit(solution)/shard_map/all_to_all | solution.py:14
  152.6 10.6 %all_to_all.45 = f32[16,2,128]{2,1,0:T(2,128)S(1)} all-to-all(f32[16,2,128]{2,1,0:T(2,128)S(1)} %broadcast_in_dim.30), channel_id=1, replica_groups=mesh['comp'=32,'feat'=16] {'feat'}, dimensions={0} | all-to-all | bytes 32768 | tf_op jit(solution)/shard_map/all_to_all | solution.py:19
  163.3 19.7 %all_to_all.46 = f32[32,2,128]{2,1,0:T(2,128)S(1)} all-to-all(f32[32,2,128]{2,1,0:T(2,128)S(1)} %broadcast_in_dim.31), channel_id=1, replica_groups=mesh['comp'=32,'feat'=16] {'comp'}, dimensions={0} | all-to-all | bytes 65536 | tf_op jit(solution)/shard_map/all_to_all | solution.py:21
  183.6 16.7 %all_gather.17 = bf16[2048,128]{1,0:T(8,128)(2,1)S(1)} all-gather(bf16[128,128]{1,0:T(8,128)(2,1)S(1)} %fusion.21), channel_id=1, replica_groups=mesh['comp'=32,'feat'=16] {'feat'}, dimensions={0}, use_global_device_ids=true | all-gather | bytes 557056 | tf_op jit(solution)/shard_map/all_gather | solution.py:66
  206.7 8.6 %collective-permute-start.1 = (f32[896,128]{1,0:T(8,128)S(1)}, f32[896,128]{1,0:T(8,128)S(1)}, u32[]{:S(2)}, u32[]{:S(2)}) collective-permute-start(f32[896,128]{1,0:T(8,128)S(1)} %constant_dynamic-slice_fusion), channel_id=1, source_target_pairs={{0,16},{16,0},{32,48},{48,32},{64,80},{80,64},{96,112},{112,96},{1... | collective-permute-start | bytes 1376264 | tf_op jit(solution)/shard_map/ppermute | solution.py:77
  217.5 3.9 %all-to-all-start.4 = ((f32[32,28,128]{2,1,0:T(8,128)}), f32[32,28,128]{2,1,0:T(8,128)S(1)}, u32[]{:S(2)}, u32[]{:S(2)}) async-start(f32[32,28,128]{2,1,0:T(8,128)} %reshape.118), calls=%async_computation.4 | async-start | bytes 1048576 | tf_op jit(solution)/shard_map/all_to_all | solution.py:79
  222.4 32.5 %all-to-all-done.4 = f32[32,28,128]{2,1,0:T(8,128)S(1)} async-done(((f32[32,28,128]{2,1,0:T(8,128)}), f32[32,28,128]{2,1,0:T(8,128)S(1)}, u32[]{:S(2)}, u32[]{:S(2)}) %all-to-all-start.4) | async-done | bytes 458784 | tf_op jit(solution)/shard_map/all_to_all | solution.py:79
  255.1 30.4 %all-gather.1 = f32[32,57,128]{2,1,0:T(8,128)S(1)} all-gather(f32[1,57,128]{2,1,0:T(8,128)S(1)} %maximum_bitcast_fusion), channel_id=2, replica_groups=mesh['comp'=32,'feat'=16] {'comp'}, dimensions={0}, use_global_device_ids=true | all-gather | bytes 963072 | tf_op jit(solution)/shard_map/all_gather | solution.py:107
  286.2 4.0 %all-to-all-start.5 = ((f32[16,1,128]{2,1,0:T(1,128)}), f32[16,1,128]{2,1,0:T(1,128)S(1)}, u32[]{:S(2)}, u32[]{:S(2)}) async-start(f32[16,1,128]{2,1,0:T(1,128)} %broadcast_in_dim.33), calls=%async_computation.5 | async-start | bytes 16384 | tf_op jit(solution)/shard_map/all_to_all | solution.py:116
  293.0 3.6 all-to-all-done.5
  299.7 3.1 convolution_bitcast_fusion
  309.7 4.3 %all-to-all-start.6 = ((f32[16,128,128]{2,1,0:T(8,128)}), f32[16,128,128]{2,1,0:T(8,128)}, u32[]{:S(2)}, u32[]{:S(2)}) async-start(f32[16,128,128]{2,1,0:T(8,128)} %copy.111), calls=%async_computation.6 | async-start | bytes 2097152 | tf_op jit(solution)/shard_map/all_to_all | solution.py:14
  315.2 14.1 %all-to-all-done.6 = f32[16,128,128]{2,1,0:T(8,128)} async-done(((f32[16,128,128]{2,1,0:T(8,128)}), f32[16,128,128]{2,1,0:T(8,128)}, u32[]{:S(2)}, u32[]{:S(2)}) %all-to-all-start.6) | async-done | bytes 1048608 | tf_op jit(solution)/shard_map/all_to_all | solution.py:14
  330.7 10.1 %all_to_all.47 = f32[16,2,128]{2,1,0:T(2,128)S(1)} all-to-all(f32[16,2,128]{2,1,0:T(2,128)S(1)} %broadcast_in_dim.34), channel_id=1, replica_groups=mesh['comp'=32,'feat'=16] {'feat'}, dimensions={0} | all-to-all | bytes 32768 | tf_op jit(solution)/shard_map/all_to_all | solution.py:19
  341.5 8.1 %all-to-all-start.8 = ((f32[32,2,128]{2,1,0:T(2,128)}), f32[32,2,128]{2,1,0:T(2,128)S(1)}, u32[]{:S(2)}, u32[]{:S(2)}) async-start(f32[32,2,128]{2,1,0:T(2,128)} %broadcast_in_dim.35), calls=%async_computation.8 | async-start | bytes 65536 | tf_op jit(solution)/shard_map/all_to_all | solution.py:21
  351.5 10.1 %all-to-all-done.8 = f32[32,2,128]{2,1,0:T(2,128)S(1)} async-done(((f32[32,2,128]{2,1,0:T(2,128)}), f32[32,2,128]{2,1,0:T(2,128)S(1)}, u32[]{:S(2)}, u32[]{:S(2)}) %all-to-all-start.8) | async-done | bytes 32800 | tf_op jit(solution)/shard_map/all_to_all | solution.py:21
  (112 shorter events, 49.3 us)
Async XLA Ops:
  0.6 23.6 %copy-start = (bf16[1,1,24,128,128]{4,3,2,1,0:T(8,128)(2,1)S(1)}, bf16[1,1,24,128,128]{4,3,2,1,0:T(8,128)(2,1)}, u32[]{:S(2)}) copy-start(bf16[1,1,24,128,128]{4,3,2,1,0:T(8,128)(2,1)} %param.10) | copy-start | bytes 2359300
  1.4 24.5 %copy-start.15 = (pred[24]{0:T(512)(128)(4,1)}, pred[24]{0:T(512)(128)(4,1)S(1)}, u32[]{:S(2)}) copy-start(pred[24]{0:T(512)(128)(4,1)S(1)} %compare_and_fusion.1) | copy-start | bytes 76
  2.7 23.2 %copy-start.7 = (s32[1024]{0:T(1024)}, s32[1024]{0:T(1024)S(1)}, u32[]{:S(2)}) copy-start(s32[1024]{0:T(1024)S(1)} %pad_clamp_fusion.1) | copy-start | bytes 12292
  25.9 2.0 copy-start.10
  29.3 11.3 %collective-permute-start = (f32[896,128]{1,0:T(8,128)S(1)}, f32[896,128]{1,0:T(8,128)S(1)}, u32[]{:S(2)}, u32[]{:S(2)}) collective-permute-start(f32[896,128]{1,0:T(8,128)S(1)} %constant_dynamic-slice_fusion.1), channel_id=1, source_target_pairs={{0,16},{16,0},{32,48},{48,32},{64,80},{80,64},{96,112},{112,96},{1... | collective-permute-start | bytes 1376264 | tf_op jit(solution)/shard_map/ppermute | solution.py:77
  41.5 47.0 %all-to-all-start = ((f32[32,28,128]{2,1,0:T(8,128)}), f32[32,28,128]{2,1,0:T(8,128)S(1)}, u32[]{:S(2)}, u32[]{:S(2)}) async-start(f32[32,28,128]{2,1,0:T(8,128)} %reshape.111), calls=%async_computation | async-start | bytes 1048576 | tf_op jit(solution)/shard_map/all_to_all | solution.py:79
  55.0 66.7 %copy-start.13 = (pred[24]{0:T(512)(128)(4,1)}, pred[24]{0:T(512)(128)(4,1)S(1)}, u32[]{:S(2)}) copy-start(pred[24]{0:T(512)(128)(4,1)S(1)} %compare_and_fusion) | copy-start | bytes 76
  118.5 0.9 copy-start.2
  120.0 4.8 %copy-start.1 = (f32[14,128,128]{2,1,0:T(8,128)}, f32[14,128,128]{2,1,0:T(8,128)S(1)}, u32[]{:S(2)}) copy-start(f32[14,128,128]{2,1,0:T(8,128)S(1)} %reshape.114) | copy-start | bytes 2752516
  124.8 3.0 copy-start.11
  131.6 51.4 %copy-start.6 = (f32[128]{0:T(128)S(1)}, f32[128]{0:T(128)}, u32[]{:S(2)}) copy-start(f32[128]{0:T(128)} %param.15) | copy-start | bytes 1540
  131.6 52.0 %copy-start.5 = (f32[128,128]{1,0:T(8,128)S(1)}, f32[128,128]{1,0:T(8,128)}, u32[]{:S(2)}) copy-start(f32[128,128]{1,0:T(8,128)} %param.14) | copy-start | bytes 196612
  131.6 20.9 %all-to-all-start.1 = ((f32[16,128,128]{2,1,0:T(8,128)}), f32[16,128,128]{2,1,0:T(8,128)S(1)}, u32[]{:S(2)}, u32[]{:S(2)}) async-start(f32[16,128,128]{2,1,0:T(8,128)} %copy.97), calls=%async_computation.1 | async-start | bytes 2097152 | tf_op jit(solution)/shard_map/all_to_all | solution.py:14
  136.4 64.6 %copy-start.16 = (pred[24]{0:T(512)(128)(4,1)S(1)}, pred[24]{0:T(512)(128)(4,1)}, u32[]{:S(2)}) copy-start(pred[24]{0:T(512)(128)(4,1)} %copy-done.15) | copy-start | bytes 76
  206.7 9.9 %collective-permute-start.1 = (f32[896,128]{1,0:T(8,128)S(1)}, f32[896,128]{1,0:T(8,128)S(1)}, u32[]{:S(2)}, u32[]{:S(2)}) collective-permute-start(f32[896,128]{1,0:T(8,128)S(1)} %constant_dynamic-slice_fusion), channel_id=1, source_target_pairs={{0,16},{16,0},{32,48},{48,32},{64,80},{80,64},{96,112},{112,96},{1... | collective-permute-start | bytes 1376264 | tf_op jit(solution)/shard_map/ppermute | solution.py:77
  217.5 37.5 %all-to-all-start.4 = ((f32[32,28,128]{2,1,0:T(8,128)}), f32[32,28,128]{2,1,0:T(8,128)S(1)}, u32[]{:S(2)}, u32[]{:S(2)}) async-start(f32[32,28,128]{2,1,0:T(8,128)} %reshape.118), calls=%async_computation.4 | async-start | bytes 1048576 | tf_op jit(solution)/shard_map/all_to_all | solution.py:79
  286.2 10.4 %all-to-all-start.5 = ((f32[16,1,128]{2,1,0:T(1,128)}), f32[16,1,128]{2,1,0:T(1,128)S(1)}, u32[]{:S(2)}, u32[]{:S(2)}) async-start(f32[16,1,128]{2,1,0:T(1,128)} %broadcast_in_dim.33), calls=%async_computation.5 | async-start | bytes 16384 | tf_op jit(solution)/shard_map/all_to_all | solution.py:116
  290.5 0.9 copy-start.3
  291.4 5.2 %copy-start.9 = (f32[2,128]{1,0:T(2,128)S(1)}, f32[2,128]{1,0:T(2,128)}, u32[]{:S(2)}) copy-start(f32[2,128]{1,0:T(2,128)} %copy-done.8) | copy-start | bytes 3076
  296.6 3.2 copy-start.14
  302.9 3.0 copy-start.12
  309.7 19.6 %all-to-all-start.6 = ((f32[16,128,128]{2,1,0:T(8,128)}), f32[16,128,128]{2,1,0:T(8,128)}, u32[]{:S(2)}, u32[]{:S(2)}) async-start(f32[16,128,128]{2,1,0:T(8,128)} %copy.111), calls=%async_computation.6 | async-start | bytes 2097152 | tf_op jit(solution)/shard_map/all_to_all | solution.py:14
  341.5 20.2 %all-to-all-start.8 = ((f32[32,2,128]{2,1,0:T(2,128)}), f32[32,2,128]{2,1,0:T(2,128)S(1)}, u32[]{:S(2)}, u32[]{:S(2)}) async-start(f32[32,2,128]{2,1,0:T(2,128)} %broadcast_in_dim.35), calls=%async_computation.8 | async-start | bytes 65536 | tf_op jit(solution)/shard_map/all_to_all | solution.py:21
  350.5 11.8 %copy-start.4 = (f32[1792,128]{1,0:T(8,128)S(1)}, f32[1792,128]{1,0:T(8,128)}, u32[]{:S(2)}) copy-start(f32[1792,128]{1,0:T(8,128)} %reshape.115) | copy-start | bytes 2752516
  (1 other events, 0.6 us)
where the time goes:
time: 366 us; the launch traced here: 365 us
  blocking collectives  137 us (37%)
  waiting for transfers between devices  113 us (31%)
  starting transfers between devices  57.1 us (16%)
  local copies, waits for them, and re-layouts  27.9 us (8%)
  matrix products  17.1 us (5%)
  other arithmetic  10.9 us (3%)
    all_to_all x2, waiting for transfers between devices, gradient_rows(): landed = lax.all_to_all(pieces, 'comp', 0, 0, tiled=True)  66 us
    all_gather x2, blocking collectives, slab_of(): lax.all_gather(current.astype(jnp.bfloat16), 'feat', axis=0, tiled=True)  36.6 us
    all_gather x1, blocking collectives, shards(): lax.all_gather(jnp.concatenate([gradient_own, col_sq(gradient_own)[None]]...  30.4 us
    all_to_all x2, waiting for transfers between devices, reduce_over(): return lax.all_to_all(pieces, axis, 0, 0, tiled=True).sum(0)  30.2 us
    all_gather x1, blocking collectives, shards(): lax.all_gather(gradient_own, 'comp', axis=0, tiled=False)  29.8 us
    all_to_all x2, blocking collectives, total_over_mesh(): by_feat = lax.all_to_all(spread, 'feat', 0, 0, tiled=True).sum(0)  20.7 us
    all_to_all x1, blocking collectives, total_over_mesh(): return lax.all_to_all(spread, 'comp', 0, 0, tiled=True).sum(0)  19.7 us
    ppermute x2, starting transfers between devices, gradient_rows(): chip_sum = kept + lax.ppermute(sent, 'comp', siblings)  18.5 us
  transfers between devices with their start and end apart: 8, of which 8 were waited for; matrix products, arithmetic and copies ran while one was open for 2% of the time, Pallas kernels for 0%

commit v1 on v0

--- a/solution.py
+++ b/solution.py
@@ -63,7 +63,12 @@
         return reduce_over(forward_summed.reshape(RB_DEV * block_edge, responses), "feat", n_feat)
 
     def slab_of(current):
-        return lax.all_gather(current.astype(jnp.bfloat16), "feat", axis=0, tiled=True)
+        return jnp.concatenate(
+            lax.all_to_all(
+                jnp.stack([current.astype(jnp.bfloat16)] * lax.axis_size("feat")), "feat", 0, 0
+            ),
+            axis=0,
+        )
 
     core = comp_index % 2
     half_rows = feat_rows // 2

time: 366 us -> 349 us (0.954)
  blocking collectives: 137 us -> 111 us
  waiting for transfers between devices: 113 us -> 122 us
    all_gather x2 -> x0, blocking collectives: 36.6 us -> none  [slab_of(): lax.all_gather(current.astype(jnp.bfloat16), 'feat', axis=0, tiled=True)]
    all_to_all x0 -> x1, blocking collectives: none -> 11.7 us  [slab_of(): lax.all_to_all(jnp.stack([current.astype(jnp.bfloat16)] * lax.axis_size('...]
    all_to_all x0 -> x1, waiting for transfers between devices: none -> 8.31 us  [slab_of(): lax.all_to_all(jnp.stack([current.astype(jnp.bfloat16)] * lax.axis_size('...]
    all_to_all x0 -> x1, starting transfers between devices: none -> 7.58 us  [slab_of(): lax.all_to_all(jnp.stack([current.astype(jnp.bfloat16)] * lax.axis_size('...]
    ppermute x2, starting transfers between devices: 18.5 us -> 11.3 us  [gradient_rows(): chip_sum = kept + lax.ppermute(sent, 'comp', siblings)]
  transfers between devices with their start and end apart: 8 -> 9, of which waited for: 8 -> 9; matrix products, arithmetic and copies ran while one was open for 2% -> 2% of each run, Pallas kernels for 0% -> 0%
where the time goes in v1:
time: 349 us; the launch traced here: 348 us
  waiting for transfers between devices  122 us (35%)
  blocking collectives  111 us (32%)
  starting transfers between devices  57.6 us (17%)
  local copies, waits for them, and re-layouts  28.9 us (8%)
  matrix products  17.1 us (5%)
  other arithmetic  9.55 us (3%)
    all_to_all x2, waiting for transfers between devices, gradient_rows(): landed = lax.all_to_all(pieces, 'comp', 0, 0, tiled=True)  66 us
    all_to_all x2, waiting for transfers between devices, reduce_over(): return lax.all_to_all(pieces, axis, 0, 0, tiled=True).sum(0)  31.5 us
    all_gather x1, blocking collectives, shards(): lax.all_gather(jnp.concatenate([gradient_own, col_sq(gradient_own)[None]]...  30.4 us
    all_gather x1, blocking collectives, shards(): lax.all_gather(gradient_own, 'comp', axis=0, tiled=False)  29.8 us
    all_to_all x2, blocking collectives, total_over_mesh(): by_feat = lax.all_to_all(spread, 'feat', 0, 0, tiled=True).sum(0)  19.7 us
    all_to_all x1, blocking collectives, total_over_mesh(): return lax.all_to_all(spread, 'comp', 0, 0, tiled=True).sum(0)  19.4 us
    all_to_all x2, starting transfers between devices, gradient_rows(): landed = lax.all_to_all(pieces, 'comp', 0, 0, tiled=True)  19 us
    all_to_all x1, blocking collectives, slab_of(): lax.all_to_all(jnp.stack([current.astype(jnp.bfloat16)] * lax.axis_size('...  11.7 us
  transfers between devices with their start and end apart: 9, of which 9 were waited for; matrix products, arithmetic and copies ran while one was open for 2% of the time, Pallas kernels for 0%

profile of v1, /device:TPU:1, one launch (start us, length us, event | category | flops | bytes accessed | tf_op | source)
XLA Modules:
  0.0 348.1 jit_solution(8098220391912056413)
XLA Ops:
  2.5 7.6 %all-to-all-start = ((bf16[16,128,128]{2,1,0:T(8,128)(2,1)}), bf16[16,128,128]{2,1,0:T(8,128)(2,1)S(1)}, u32[]{:S(2)}, u32[]{:S(2)}) async-start(bf16[16,128,128]{2,1,0:T(8,128)(2,1)} %stack.16), calls=%async_computation | async-start | bytes 1048576 | tf_op jit(solution)/shard_map/all_to_all | solution.py:67
  10.8 8.3 %all-to-all-done = bf16[16,128,128]{2,1,0:T(8,128)(2,1)S(1)} async-done(((bf16[16,128,128]{2,1,0:T(8,128)(2,1)}), bf16[16,128,128]{2,1,0:T(8,128)(2,1)S(1)}, u32[]{:S(2)}, u32[]{:S(2)}) %all-to-all-start) | async-done | bytes 524320 | tf_op jit(solution)/shard_map/all_to_all | solution.py:67
  24.9 5.8 %collective-permute-start = (f32[896,128]{1,0:T(8,128)S(1)}, f32[896,128]{1,0:T(8,128)S(1)}, u32[]{:S(2)}, u32[]{:S(2)}) collective-permute-start(f32[896,128]{1,0:T(8,128)S(1)} %constant_dynamic-slice_fusion.1), channel_id=1, source_target_pairs={{0,16},{16,0},{32,48},{48,32},{64,80},{80,64},{96,112},{112,96},{1... | collective-permute-start | bytes 1376264 | tf_op jit(solution)/shard_map/ppermute | solution.py:82
  33.0 15.1 %all-to-all-start.1 = ((f32[32,28,128]{2,1,0:T(8,128)}), f32[32,28,128]{2,1,0:T(8,128)S(1)}, u32[]{:S(2)}, u32[]{:S(2)}) async-start(f32[32,28,128]{2,1,0:T(8,128)} %reshape.108), calls=%async_computation.1 | async-start | bytes 1048576 | tf_op jit(solution)/shard_map/all_to_all | solution.py:84
  48.2 33.5 %all-to-all-done.1 = f32[32,28,128]{2,1,0:T(8,128)S(1)} async-done(((f32[32,28,128]{2,1,0:T(8,128)}), f32[32,28,128]{2,1,0:T(8,128)S(1)}, u32[]{:S(2)}, u32[]{:S(2)}) %all-to-all-start.1) | async-done | bytes 458784 | tf_op jit(solution)/shard_map/all_to_all | solution.py:84
  81.7 29.8 %all_gather.9 = f32[32,56,128]{2,1,0:T(8,128)S(1)} all-gather(f32[1,56,128]{2,1,0:T(8,128)S(1)} %all_gather_reshape.3), channel_id=1, replica_groups=mesh['comp'=32,'feat'=16] {'comp'}, dimensions={0}, use_global_device_ids=true | all-gather | bytes 946176 | tf_op jit(solution)/shard_map/all_gather | solution.py:102
  114.8 3.1 convolution_bitcast_fusion.2
  124.7 3.8 %all-to-all-start.2 = ((f32[16,128,128]{2,1,0:T(8,128)}), f32[16,128,128]{2,1,0:T(8,128)S(1)}, u32[]{:S(2)}, u32[]{:S(2)}) async-start(f32[16,128,128]{2,1,0:T(8,128)} %copy.97), calls=%async_computation.2 | async-start | bytes 2097152 | tf_op jit(solution)/shard_map/all_to_all | solution.py:14
  128.6 17.4 %all-to-all-done.2 = f32[16,128,128]{2,1,0:T(8,128)S(1)} async-done(((f32[16,128,128]{2,1,0:T(8,128)}), f32[16,128,128]{2,1,0:T(8,128)S(1)}, u32[]{:S(2)}, u32[]{:S(2)}) %all-to-all-start.2) | async-done | bytes 1048608 | tf_op jit(solution)/shard_map/all_to_all | solution.py:14
  146.0 9.5 %all_to_all.55 = f32[16,2,128]{2,1,0:T(2,128)S(1)} all-to-all(f32[16,2,128]{2,1,0:T(2,128)S(1)} %broadcast_in_dim.30), channel_id=1, replica_groups=mesh['comp'=32,'feat'=16] {'feat'}, dimensions={0} | all-to-all | bytes 32768 | tf_op jit(solution)/shard_map/all_to_all | solution.py:19
  155.6 19.4 %all_to_all.56 = f32[32,2,128]{2,1,0:T(2,128)S(1)} all-to-all(f32[32,2,128]{2,1,0:T(2,128)S(1)} %broadcast_in_dim.31), channel_id=1, replica_groups=mesh['comp'=32,'feat'=16] {'comp'}, dimensions={0} | all-to-all | bytes 65536 | tf_op jit(solution)/shard_map/all_to_all | solution.py:21
  175.7 11.7 %all_to_all.57 = bf16[16,128,128]{2,1,0:T(8,128)(2,1)S(1)} all-to-all(bf16[16,128,128]{2,1,0:T(8,128)(2,1)S(1)} %stack.20), channel_id=1, replica_groups=mesh['comp'=32,'feat'=16] {'feat'}, dimensions={0} | all-to-all | bytes 1048576 | tf_op jit(solution)/shard_map/all_to_all | solution.py:67
  194.0 5.5 %collective-permute-start.1 = (f32[896,128]{1,0:T(8,128)S(1)}, f32[896,128]{1,0:T(8,128)S(1)}, u32[]{:S(2)}, u32[]{:S(2)}) collective-permute-start(f32[896,128]{1,0:T(8,128)S(1)} %constant_dynamic-slice_fusion), channel_id=1, source_target_pairs={{0,16},{16,0},{32,48},{48,32},{64,80},{80,64},{96,112},{112,96},{1... | collective-permute-start | bytes 1376264 | tf_op jit(solution)/shard_map/ppermute | solution.py:82
  201.6 3.9 %all-to-all-start.6 = ((f32[32,28,128]{2,1,0:T(8,128)}), f32[32,28,128]{2,1,0:T(8,128)S(1)}, u32[]{:S(2)}, u32[]{:S(2)}) async-start(f32[32,28,128]{2,1,0:T(8,128)} %reshape.114), calls=%async_computation.6 | async-start | bytes 1048576 | tf_op jit(solution)/shard_map/all_to_all | solution.py:84
  206.5 32.5 %all-to-all-done.6 = f32[32,28,128]{2,1,0:T(8,128)S(1)} async-done(((f32[32,28,128]{2,1,0:T(8,128)}), f32[32,28,128]{2,1,0:T(8,128)S(1)}, u32[]{:S(2)}, u32[]{:S(2)}) %all-to-all-start.6) | async-done | bytes 458784 | tf_op jit(solution)/shard_map/all_to_all | solution.py:84
  239.2 30.4 %all-gather.1 = f32[32,57,128]{2,1,0:T(8,128)S(1)} all-gather(f32[1,57,128]{2,1,0:T(8,128)S(1)} %maximum_bitcast_fusion), channel_id=2, replica_groups=mesh['comp'=32,'feat'=16] {'comp'}, dimensions={0}, use_global_device_ids=true | all-gather | bytes 963072 | tf_op jit(solution)/shard_map/all_gather | solution.py:112
  270.3 3.5 all-to-all-start.7
  276.5 3.5 %all-to-all-done.7 = f32[16,1,128]{2,1,0:T(1,128)S(1)} async-done(((f32[16,1,128]{2,1,0:T(1,128)}), f32[16,1,128]{2,1,0:T(1,128)S(1)}, u32[]{:S(2)}, u32[]{:S(2)}) %all-to-all-start.7) | async-done | bytes 8224 | tf_op jit(solution)/shard_map/all_to_all | solution.py:121
  283.2 3.1 convolution_bitcast_fusion
  293.2 4.3 %all-to-all-start.8 = ((f32[16,128,128]{2,1,0:T(8,128)}), f32[16,128,128]{2,1,0:T(8,128)}, u32[]{:S(2)}, u32[]{:S(2)}) async-start(f32[16,128,128]{2,1,0:T(8,128)} %copy.111), calls=%async_computation.8 | async-start | bytes 2097152 | tf_op jit(solution)/shard_map/all_to_all | solution.py:14
  298.7 14.1 %all-to-all-done.8 = f32[16,128,128]{2,1,0:T(8,128)} async-done(((f32[16,128,128]{2,1,0:T(8,128)}), f32[16,128,128]{2,1,0:T(8,128)}, u32[]{:S(2)}, u32[]{:S(2)}) %all-to-all-start.8) | async-done | bytes 1048608 | tf_op jit(solution)/shard_map/all_to_all | solution.py:14
  314.1 10.2 %all_to_all.58 = f32[16,2,128]{2,1,0:T(2,128)S(1)} all-to-all(f32[16,2,128]{2,1,0:T(2,128)S(1)} %broadcast_in_dim.34), channel_id=1, replica_groups=mesh['comp'=32,'feat'=16] {'feat'}, dimensions={0} | all-to-all | bytes 32768 | tf_op jit(solution)/shard_map/all_to_all | solution.py:19
  325.0 8.1 %all-to-all-start.10 = ((f32[32,2,128]{2,1,0:T(2,128)}), f32[32,2,128]{2,1,0:T(2,128)S(1)}, u32[]{:S(2)}, u32[]{:S(2)}) async-start(f32[32,2,128]{2,1,0:T(2,128)} %broadcast_in_dim.35), calls=%async_computation.10 | async-start | bytes 65536 | tf_op jit(solution)/shard_map/all_to_all | solution.py:21
  335.0 10.1 %all-to-all-done.10 = f32[32,2,128]{2,1,0:T(2,128)S(1)} async-done(((f32[32,2,128]{2,1,0:T(2,128)}), f32[32,2,128]{2,1,0:T(2,128)S(1)}, u32[]{:S(2)}, u32[]{:S(2)}) %all-to-all-start.10) | async-done | bytes 32800 | tf_op jit(solution)/shard_map/all_to_all | solution.py:21
  (115 shorter events, 51.9 us)
Async XLA Ops:
  0.6 19.2 %copy-start = (bf16[1,1,24,128,128]{4,3,2,1,0:T(8,128)(2,1)S(1)}, bf16[1,1,24,128,128]{4,3,2,1,0:T(8,128)(2,1)}, u32[]{:S(2)}) copy-start(bf16[1,1,24,128,128]{4,3,2,1,0:T(8,128)(2,1)} %param.10) | copy-start | bytes 2359300
  0.6 9.4 %copy-start.11 = (s32[1,1,24]{2,1,0:T(1,128)S(1)}, s32[1,1,24]{2,1,0:T(1,128)}, u32[]{:S(2)}) copy-start(s32[1,1,24]{2,1,0:T(1,128)} %param.11) | copy-start | bytes 292
  2.5 16.7 %all-to-all-start = ((bf16[16,128,128]{2,1,0:T(8,128)(2,1)}), bf16[16,128,128]{2,1,0:T(8,128)(2,1)S(1)}, u32[]{:S(2)}, u32[]{:S(2)}) async-start(bf16[16,128,128]{2,1,0:T(8,128)(2,1)} %stack.16), calls=%async_computation | async-start | bytes 1048576 | tf_op jit(solution)/shard_map/all_to_all | solution.py:67
  10.8 10.7 %copy-start.7 = (s32[1024]{0:T(1024)}, s32[1024]{0:T(1024)S(1)}, u32[]{:S(2)}) copy-start(s32[1024]{0:T(1024)S(1)} %pad_clamp_fusion.1) | copy-start | bytes 12292
  10.8 10.7 %copy-start.15 = (pred[24]{0:T(512)(128)(4,1)}, pred[24]{0:T(512)(128)(4,1)S(1)}, u32[]{:S(2)}) copy-start(pred[24]{0:T(512)(128)(4,1)S(1)} %compare_and_fusion.1) | copy-start | bytes 76
  21.5 2.0 copy-start.10
  24.9 7.2 %collective-permute-start = (f32[896,128]{1,0:T(8,128)S(1)}, f32[896,128]{1,0:T(8,128)S(1)}, u32[]{:S(2)}, u32[]{:S(2)}) collective-permute-start(f32[896,128]{1,0:T(8,128)S(1)} %constant_dynamic-slice_fusion.1), channel_id=1, source_target_pairs={{0,16},{16,0},{32,48},{48,32},{64,80},{80,64},{96,112},{112,96},{1... | collective-permute-start | bytes 1376264 | tf_op jit(solution)/shard_map/ppermute | solution.py:82
  33.0 48.7 %all-to-all-start.1 = ((f32[32,28,128]{2,1,0:T(8,128)}), f32[32,28,128]{2,1,0:T(8,128)S(1)}, u32[]{:S(2)}, u32[]{:S(2)}) async-start(f32[32,28,128]{2,1,0:T(8,128)} %reshape.108), calls=%async_computation.1 | async-start | bytes 1048576 | tf_op jit(solution)/shard_map/all_to_all | solution.py:84
  48.1 66.7 %copy-start.13 = (pred[24]{0:T(512)(128)(4,1)}, pred[24]{0:T(512)(128)(4,1)S(1)}, u32[]{:S(2)}) copy-start(pred[24]{0:T(512)(128)(4,1)S(1)} %compare_and_fusion) | copy-start | bytes 76
  113.2 4.8 %copy-start.1 = (f32[14,128,128]{2,1,0:T(8,128)}, f32[14,128,128]{2,1,0:T(8,128)S(1)}, u32[]{:S(2)}) copy-start(f32[14,128,128]{2,1,0:T(8,128)S(1)} %reshape.111) | copy-start | bytes 2752516
  124.7 50.3 %copy-start.6 = (f32[128]{0:T(128)S(1)}, f32[128]{0:T(128)}, u32[]{:S(2)}) copy-start(f32[128]{0:T(128)} %param.15) | copy-start | bytes 1540
  124.7 50.3 %copy-start.5 = (f32[128,128]{1,0:T(8,128)S(1)}, f32[128,128]{1,0:T(8,128)}, u32[]{:S(2)}) copy-start(f32[128,128]{1,0:T(8,128)} %param.14) | copy-start | bytes 196612
  124.7 21.2 %all-to-all-start.2 = ((f32[16,128,128]{2,1,0:T(8,128)}), f32[16,128,128]{2,1,0:T(8,128)S(1)}, u32[]{:S(2)}, u32[]{:S(2)}) async-start(f32[16,128,128]{2,1,0:T(8,128)} %copy.97), calls=%async_computation.2 | async-start | bytes 2097152 | tf_op jit(solution)/shard_map/all_to_all | solution.py:14
  175.6 12.7 %copy-start.16 = (pred[24]{0:T(512)(128)(4,1)S(1)}, pred[24]{0:T(512)(128)(4,1)}, u32[]{:S(2)}) copy-start(pred[24]{0:T(512)(128)(4,1)} %copy-done.15) | copy-start | bytes 76
  194.0 6.8 %collective-permute-start.1 = (f32[896,128]{1,0:T(8,128)S(1)}, f32[896,128]{1,0:T(8,128)S(1)}, u32[]{:S(2)}, u32[]{:S(2)}) collective-permute-start(f32[896,128]{1,0:T(8,128)S(1)} %constant_dynamic-slice_fusion), channel_id=1, source_target_pairs={{0,16},{16,0},{32,48},{48,32},{64,80},{80,64},{96,112},{112,96},{1... | collective-permute-start | bytes 1376264 | tf_op jit(solution)/shard_map/ppermute | solution.py:82
  201.6 37.5 %all-to-all-start.6 = ((f32[32,28,128]{2,1,0:T(8,128)}), f32[32,28,128]{2,1,0:T(8,128)S(1)}, u32[]{:S(2)}, u32[]{:S(2)}) async-start(f32[32,28,128]{2,1,0:T(8,128)} %reshape.114), calls=%async_computation.6 | async-start | bytes 1048576 | tf_op jit(solution)/shard_map/all_to_all | solution.py:84
  270.3 9.8 %all-to-all-start.7 = ((f32[16,1,128]{2,1,0:T(1,128)}), f32[16,1,128]{2,1,0:T(1,128)S(1)}, u32[]{:S(2)}, u32[]{:S(2)}) async-start(f32[16,1,128]{2,1,0:T(1,128)} %broadcast_in_dim.33), calls=%async_computation.7 | async-start | bytes 16384 | tf_op jit(solution)/shard_map/all_to_all | solution.py:121
  274.0 0.9 copy-start.3
  274.9 5.1 %copy-start.9 = (f32[2,128]{1,0:T(2,128)S(1)}, f32[2,128]{1,0:T(2,128)}, u32[]{:S(2)}) copy-start(f32[2,128]{1,0:T(2,128)} %copy-done.8) | copy-start | bytes 3076
  280.1 3.2 copy-start.14
  286.3 3.0 copy-start.12
  293.2 19.6 %all-to-all-start.8 = ((f32[16,128,128]{2,1,0:T(8,128)}), f32[16,128,128]{2,1,0:T(8,128)}, u32[]{:S(2)}, u32[]{:S(2)}) async-start(f32[16,128,128]{2,1,0:T(8,128)} %copy.111), calls=%async_computation.8 | async-start | bytes 2097152 | tf_op jit(solution)/shard_map/all_to_all | solution.py:14
  325.0 20.2 %all-to-all-start.10 = ((f32[32,2,128]{2,1,0:T(2,128)}), f32[32,2,128]{2,1,0:T(2,128)S(1)}, u32[]{:S(2)}, u32[]{:S(2)}) async-start(f32[32,2,128]{2,1,0:T(2,128)} %broadcast_in_dim.35), calls=%async_computation.10 | async-start | bytes 65536 | tf_op jit(solution)/shard_map/all_to_all | solution.py:21
  334.0 11.8 %copy-start.4 = (f32[1792,128]{1,0:T(8,128)S(1)}, f32[1792,128]{1,0:T(8,128)}, u32[]{:S(2)}) copy-start(f32[1792,128]{1,0:T(8,128)} %reshape.112) | copy-start | bytes 2752516
  (2 other events, 1.5 us)
